TPU v7x, 256 devices: a whole 4x4x8 slice. The times are simulated.
256 devices in a mesh: gx: 16 (over y_lo, z), gy: 4 (over y_hi, core), gz: 4 (over x).
Axes of the slice: x: 4, y: 4 (y_hi: 2, y_lo: 2; y = y_hi * 2 + y_lo), z: 8, core: 2. Of those that a mesh axis runs over, the one named last changes fastest.
Arguments:
- velocity: float32 [3, 64, 32, 1024], P(None, 'gx', 'gy', 'gz'), may hold values from -6 to 6
- stress: float32 [6, 64, 32, 1024], P(None, 'gx', 'gy', 'gz'), may hold values from -6 to 6
- buoyancy: float32 [64, 32, 1024], P('gx', 'gy', 'gz'), may hold values from 0.5 to 1
- lame_lambda: float32 [64, 32, 1024], P('gx', 'gy', 'gz'), may hold values from 0.5 to 1.5
- shear_modulus: float32 [64, 32, 1024], P('gx', 'gy', 'gz'), may hold values from 0.3 to 1
- slip_rate: bfloat16 [2048, 4096], P(('gx', 'gy', 'gz')), may hold values from 0 to 2
- taps: bfloat16 [512], replicated, may hold values from -0.25 to 0.25
- moment: float32 [6, 2048], P(None, ('gx', 'gy', 'gz')), may hold values from -6 to 6
- cells: int32 [3, 2048], replicated, may hold values from 0 to 511, as said below
- onsets: int32 [2048], P(('gx', 'gy', 'gz')), may hold values from 0 to 2624, as said below
Outputs:
- velocity_out: float32 [3, 64, 32, 1024], P(None, 'gx', 'gy', 'gz')
- stress_out: float32 [6, 64, 32, 1024], P(None, 'gx', 'gy', 'gz')
Inputs may be any that keep to these rules, and one draw needn't show every extreme that they name: `cells`: row 0 is below 64, row 1 is 15 or 16, row 2 is below 512. `onsets`: every subfault's frames lie inside its slip-rate function.
All inputs are finite; a program needn't handle non-finite values.
Results may differ from a plain program's by a relative error of at most 0.0003.
Values sent between devices are 32-bit elements; how exact they have to be, the bound alone decides.
No kernel may reach another device: no remote copies, remote signals or barrier semaphores. Data moves between devices by JAX's collectives and lax.ppermute only.
A program may use at most 64 MiB of HBM per device.

v0:
```python
import jax
import jax.numpy as jnp
from jax import lax
from jax.sharding import PartitionSpec as P

TAPS = 512
HOP = 64
STEPS = 16
STEP_TIME = 0.25


def with_halo(block, sides, width):
    for axis, dim in sides:
        count = lax.axis_size(axis)
        forward = [(i, i + 1) for i in range(count - 1)]
        backward = [(target, source) for source, target in forward]
        low = lax.ppermute(
            lax.slice_in_dim(block, block.shape[dim] - width, None, axis=dim), axis, forward
        )
        high = lax.ppermute(lax.slice_in_dim(block, 0, width, axis=dim), axis, backward)
        block = jnp.concatenate([low, block, high], axis=dim)
    return block


def window(array, axis, offset):
    cuts = [slice(None)] * (array.ndim - 3)
    for dim in range(3):
        extent = array.shape[array.ndim - 3 + dim]
        if dim == axis:
            cuts.append(slice(1 + offset, extent - 1 + offset))
        else:
            cuts.append(slice(1, extent - 1))
    return array[tuple(cuts)]


def forward(array, axis):
    return window(array, axis, 1) - window(array, axis, 0)


def backward(array, axis):
    return window(array, axis, 0) - window(array, axis, -1)


def velocity_update(stress_pad, velocity, buoyancy):
    factor = STEP_TIME * buoyancy
    velocity_x = velocity[0] + factor * (
        forward(stress_pad[0], 0) + backward(stress_pad[3], 1) + backward(stress_pad[4], 2)
    )
    velocity_y = velocity[1] + factor * (
        backward(stress_pad[3], 0) + forward(stress_pad[1], 1) + backward(stress_pad[5], 2)
    )
    velocity_z = velocity[2] + factor * (
        backward(stress_pad[4], 0) + backward(stress_pad[5], 1) + forward(stress_pad[2], 2)
    )
    return jnp.stack([velocity_x, velocity_y, velocity_z])


def stress_update(velocity_pad, stress, lame_lambda, shear_modulus):
    strain_x = backward(velocity_pad[0], 0)
    strain_y = backward(velocity_pad[1], 1)
    strain_z = backward(velocity_pad[2], 2)
    stiffness = lame_lambda + 2.0 * shear_modulus
    normal_x = stress[0] + STEP_TIME * (stiffness * strain_x + lame_lambda * (strain_y + strain_z))
    normal_y = stress[1] + STEP_TIME * (stiffness * strain_y + lame_lambda * (strain_x + strain_z))
    normal_z = stress[2] + STEP_TIME * (stiffness * strain_z + lame_lambda * (strain_x + strain_y))
    shear_xy = stress[3] + STEP_TIME * shear_modulus * (
        forward(velocity_pad[0], 1) + forward(velocity_pad[1], 0)
    )
    shear_xz = stress[4] + STEP_TIME * shear_modulus * (
        forward(velocity_pad[0], 2) + forward(velocity_pad[2], 0)
    )
    shear_yz = stress[5] + STEP_TIME * shear_modulus * (
        forward(velocity_pad[1], 2) + forward(velocity_pad[2], 1)
    )
    return jnp.stack([normal_x, normal_y, normal_z, shear_xy, shear_xz, shear_yz])


def build_frames(slip_rate, onsets):
    span = HOP * (STEPS - 1) + TAPS
    offsets = (
        HOP * jnp.arange(STEPS, dtype=jnp.int32)[:, None]
        + jnp.arange(TAPS, dtype=jnp.int32)[None, :]
    )

    def frames_of(row, start):
        return lax.dynamic_slice_in_dim(row, start, span)[offsets]

    return jax.vmap(frames_of)(slip_rate, onsets)


def on_device(
    velocity, stress, buoyancy, lame_lambda, shear_modulus, slip_rate, taps, moment, cells, onsets
):
    frames = build_frames(slip_rate, onsets)
    rates = jnp.einsum("fnk,k->nf", frames, taps, preferred_element_type=jnp.float32)
    local_rate = moment[:, None, :] * rates[None, :, :]
    moment_rate = lax.all_gather(local_rate, ("gx", "gy", "gz"), axis=2, tiled=True)
    width_x, width_y, width_z = buoyancy.shape
    local_x = cells[0] - lax.axis_index("gx") * width_x
    local_y = cells[1] - lax.axis_index("gy") * width_y
    local_z = cells[2] - lax.axis_index("gz") * width_z
    inside = (
        (local_x >= 0)
        & (local_x < width_x)
        & (local_y >= 0)
        & (local_y < width_y)
        & (local_z >= 0)
        & (local_z < width_z)
    )
    local_x = jnp.where(inside, local_x, width_x)
    local_y = jnp.where(inside, local_y, width_y)
    local_z = jnp.where(inside, local_z, width_z)

    def inject(stress_now, step):
        source = lax.dynamic_index_in_dim(moment_rate, step, 1, keepdims=False)
        return stress_now.at[:, local_x, local_y, local_z].add(-STEP_TIME * source, mode="drop")

    def advance(step, carry):
        velocity_now, stress_now = carry
        stress_pad = with_halo(stress_now, (("gx", 1), ("gy", 2), ("gz", 3)), 1)
        velocity_now = velocity_update(stress_pad, velocity_now, buoyancy)
        velocity_pad = with_halo(velocity_now, (("gx", 1), ("gy", 2), ("gz", 3)), 1)
        stress_now = stress_update(velocity_pad, stress_now, lame_lambda, shear_modulus)
        return (velocity_now, inject(stress_now, step))

    velocity_out, stress_out = lax.fori_loop(0, STEPS, advance, (velocity, stress))
    return (velocity_out, stress_out)


def solution(mesh):
    placed = (
        P(None, "gx", "gy", "gz"),
        P(None, "gx", "gy", "gz"),
        P("gx", "gy", "gz"),
        P("gx", "gy", "gz"),
        P("gx", "gy", "gz"),
        P(("gx", "gy", "gz"), None),
        P(),
        P(None, ("gx", "gy", "gz")),
        P(),
        P(("gx", "gy", "gz")),
    )
    return jax.shard_map(
        on_device,
        mesh=mesh,
        in_specs=placed,
        out_specs=(P(None, "gx", "gy", "gz"), P(None, "gx", "gy", "gz")),
        check_vma=False,
    )
```

profile of v0, /device:TPU:30, one launch (start us, length us, event | category | flops | bytes accessed | tf_op | source)
XLA Modules:
  0.0 2108.1 jit_solution(9288432710862921413)
XLA Ops:
  3.7 23.6 %while.17 = (s32[]{:T(128)}, bf16[8,4096]{1,0:T(8,128)(2,1)}, s32[8,2]{0,1:T(2,128)S(1)}, bf16[8,1472]{1,0:T(8,128)(2,1)S(1)}, s32[]{:T(128)}, /*index=5*/s32[]{:T(128)}) while((s32[]{:T(128)}, bf16[8,4096]{1,0:T(8,128)(2,1)}, s32[8,2]{0,1:T(2,128)S(1)}, bf16[8,1472]{1,0:T(8,128)(2,1)S(1)}, s32[]{:T(128)}, /*index=5*/s32[]{:T(128)}) %tuple.89), condition=%wide.while_cond, body=%wide.while_body.sunk | while | flops 2 | bytes 11897 | solution.py:86
  27.7 24.0 %gather_fusion = bf16[8192,8]{1,0:T(8,128)(2,1)S(1)} fusion(bf16[8,1472]{0,1:T(8,128)(2,1)S(1)} %copy.37, s32[8192]{0:T(1024)S(1)} %broadcast_clamp_fusion), kind=kCustom, calls=%fused_computation | custom fusion | bytes 294912 | tf_op jit(solution)/shard_map/vmap()/gather | solution.py:86
  55.0 680.8 %all_gather.3 = f32[6,16,2048]{0,2,1:T(8,128)} all-gather(f32[6,16,8]{0,2,1:T(8,128)S(1)} %broadcast_multiply_fusion), channel_id=1, replica_groups=mesh['gx'=16,'gy'=4,'gz'=4] {'gx','gy','gz'}, dimensions={2}, use_global_device_ids=true | all-gather | bytes 789504 | tf_op jit(solution)/shard_map/all_gather | solution.py:97
  735.8 1368.8 %while.16 = (s32[]{:T(128)}, f32[3,4,8,256]{3,2,1,0:T(8,128)S(1)}, f32[6,4,8,256]{0,3,2,1:T(8,128)}, f32[4,8,256]{2,1,0:T(8,128)S(1)}, f32[4,8,256]{2,1,0:T(8,12...) while((s32[]{:T(128)}, f32[3,4,8,256]{3,2,1,0:T(8,128)S(1)}, ...), condition=%wide.region_2.3_spmd, body=%wide.region_0.2_spmd.sunk | while | flops 2405409 | bytes 10088273 | solution.py:126
  740.7 7.0 collective-permute-start.1
  754.5 8.8 collective-permute-start.3
  763.3 5.7 collective-permute-done.3
  769.2 6.1 collective-permute-start.4
  779.5 4.4 collective-permute-done.5
  785.0 38.0 %collective-permute-start.6 = (f32[3,1,8,256]{3,2,1,0:T(8,128)S(1)}, f32[3,1,8,256]{3,2,1,0:T(8,128)S(1)}, u32[]{:S(2)}, u32[]{:S(2)}) collective-permute-start(f32[3,1,8,256]{3,2,1,0:T(8,128)S(1)} %get-tuple-element.391), channel_id=1, source_target_pairs={{16,0},{32,16},{48,32},{64,48},{80,64},{96,80},{112,96},{128,112},... | collective-permute-start | bytes 73736 | tf_op jit(solution)/shard_map/while/body/eval_jaxpr/ppermute | solution.py:20
  825.0 41.4 %collective-permute-done.7 = f32[3,1,8,256]{3,2,1,0:T(8,128)S(1)} collective-permute-done((f32[3,1,8,256]{3,2,1,0:T(8,128)S(1)}, f32[3,1,8,256]{3,2,1,0:T(8,128)S(1)}, u32[]{:S(2)}, u32[]{:S(2)}) %collective-permute-start.7) | collective-permute-done | bytes 24608 | tf_op jit(solution)/shard_map/while/body/eval_jaxpr/ppermute | solution.py:17
  871.1 4.5 collective-permute-done.9
  875.8 5.9 collective-permute-start.10
  884.3 4.4 collective-permute-done.11
  892.5 14.9 scatter_custom_fusion.5
  916.2 5.4 collective-permute-done.1
  938.8 4.4 collective-permute-done.5
  975.4 14.9 scatter_custom_fusion.5
  1018.4 4.4 collective-permute-done.5
  1055.0 14.9 scatter_custom_fusion.5
  1098.0 4.4 collective-permute-done.5
  1134.6 14.9 scatter_custom_fusion.5
  1177.5 4.4 collective-permute-done.5
  1214.2 14.9 scatter_custom_fusion.5
  1257.1 4.4 collective-permute-done.5
  1293.8 14.9 scatter_custom_fusion.5
  1336.7 4.4 collective-permute-done.5
  1373.4 14.9 scatter_custom_fusion.5
  1416.3 4.4 collective-permute-done.5
  1444.8 4.4 collective-permute-done.11
  1452.9 14.9 scatter_custom_fusion.5
  1495.9 4.4 collective-permute-done.5
  1532.5 14.9 scatter_custom_fusion.5
  1575.5 4.4 collective-permute-done.5
  1612.1 14.9 scatter_custom_fusion.5
  1655.1 4.4 collective-permute-done.5
  1691.7 14.9 scatter_custom_fusion.5
  1734.7 4.4 collective-permute-done.5
  1771.3 14.9 scatter_custom_fusion.5
  1814.3 4.4 collective-permute-done.5
  1850.9 14.9 scatter_custom_fusion.5
  1893.9 4.4 collective-permute-done.5
  1922.4 4.4 collective-permute-done.11
  1930.5 14.9 scatter_custom_fusion.5
  1973.5 4.4 collective-permute-done.5
  2010.1 14.9 scatter_custom_fusion.5
  2053.1 4.4 collective-permute-done.5
  2089.7 14.9 scatter_custom_fusion.5
  (870 shorter events, 953.3 us)
Async XLA Ops:
  738.8 9.1 collective-permute-start
  740.7 11.1 collective-permute-start.1
  751.8 11.5 collective-permute-start.2
  754.5 14.5 collective-permute-start.3
  769.2 10.3 collective-permute-start.4
  775.3 8.6 collective-permute-start.5
  785.0 40.1 %collective-permute-start.6 = (f32[3,1,8,256]{3,2,1,0:T(8,128)S(1)}, f32[3,1,8,256]{3,2,1,0:T(8,128)S(1)}, u32[]{:S(2)}, u32[]{:S(2)}) collective-permute-start(f32[3,1,8,256]{3,2,1,0:T(8,128)S(1)} %get-tuple-element.391), channel_id=1, source_target_pairs={{16,0},{32,16},{48,32},{64,48},{80,64},{96,80},{112,96},{128,112},... | collective-permute-start | bytes 73736 | tf_op jit(solution)/shard_map/while/body/eval_jaxpr/ppermute | solution.py:20
  823.0 43.4 %collective-permute-start.7 = (f32[3,1,8,256]{3,2,1,0:T(8,128)S(1)}, f32[3,1,8,256]{3,2,1,0:T(8,128)S(1)}, u32[]{:S(2)}, u32[]{:S(2)}) collective-permute-start(f32[3,1,8,256]{3,2,1,0:T(8,128)S(1)} %get-tuple-element.392), channel_id=1, source_target_pairs={{0,16},{16,32},{32,48},{48,64},{64,80},{80,96},{96,112},{112,128},... | collective-permute-start | bytes 73736 | tf_op jit(solution)/shard_map/while/body/eval_jaxpr/ppermute | solution.py:17
  875.8 8.5 collective-permute-start.10
  913.6 8.1 collective-permute-start.1
  930.7 8.1 collective-permute-start.4
  934.6 8.6 collective-permute-start.5
  946.1 7.8 collective-permute-start.7
  995.1 8.1 collective-permute-start.1
  1014.2 8.6 collective-permute-start.5
  1025.7 7.8 collective-permute-start.7
  1074.7 8.1 collective-permute-start.1
  1093.7 8.6 collective-permute-start.5
  1105.3 7.8 collective-permute-start.7
  1154.3 8.1 collective-permute-start.1
  1173.3 8.6 collective-permute-start.5
  1184.9 7.8 collective-permute-start.7
  1233.9 8.1 collective-permute-start.1
  1252.9 8.6 collective-permute-start.5
  1264.5 7.8 collective-permute-start.7
  1313.5 8.1 collective-permute-start.1
  1332.5 8.6 collective-permute-start.5
  1344.1 7.8 collective-permute-start.7
  1393.1 8.1 collective-permute-start.1
  1412.1 8.6 collective-permute-start.5
  1423.7 7.8 collective-permute-start.7
  1472.7 8.1 collective-permute-start.1
  1491.7 8.6 collective-permute-start.5
  1503.3 7.8 collective-permute-start.7
  1552.3 8.1 collective-permute-start.1
  1571.3 8.6 collective-permute-start.5
  1631.9 8.1 collective-permute-start.1
  1650.9 8.6 collective-permute-start.5
  1711.5 8.1 collective-permute-start.1
  1730.5 8.6 collective-permute-start.5
  1791.1 8.1 collective-permute-start.1
  1810.1 8.6 collective-permute-start.5
  1870.6 8.1 collective-permute-start.1
  1889.7 8.6 collective-permute-start.5
  1950.2 8.1 collective-permute-start.1
  1969.3 8.6 collective-permute-start.5
  2029.8 8.1 collective-permute-start.1
  2048.9 8.6 collective-permute-start.5
  (152 other events, 4985.3 us)
where the time goes:
time: 2120 us; the launch traced here: 2110 us
  blocking collectives  681 us (32%)
  waiting for transfers between devices  511 us (24%)
  starting transfers between devices  483 us (23%)
  other arithmetic  278 us (13%)
  local copies, waits for them, and re-layouts  150 us (7%)
    all_gather x1, blocking collectives, on_device(): lax.all_gather(local_rate, ('gx', 'gy', 'gz'), axis=2, tiled=True)  681 us
    ppermute x96, waiting for transfers between devices, with_halo(): lax.ppermute(lax.slice_in_dim(block, block.shape[dim] - width, None, axis...  441 us
    while x144, other arithmetic  250 us
    ppermute x96, starting transfers between devices, with_halo(): lax.ppermute(lax.slice_in_dim(block, block.shape[dim] - width, None, axis...  249 us
    ppermute x96, starting transfers between devices, with_halo(): lax.ppermute(lax.slice_in_dim(block, 0, width, axis=dim), axis, backward)  233 us
    ppermute x96, waiting for transfers between devices, with_halo(): lax.ppermute(lax.slice_in_dim(block, 0, width, axis=dim), axis, backward)  69.7 us
    another operation x16, local copies, waits for them, and re-layouts  46.3 us
    another operation x16, local copies, waits for them, and re-layouts, stress_update(): jnp.stack([normal_x, normal_y, normal_z, shear_xy, shear_xz, shear_yz])  42.5 us
  transfers between devices with their start and end apart: 192, of which 144 were waited for; matrix products, arithmetic and copies ran while one was open for 0% of the time, Pallas kernels for 0%

commit v1 on v0

--- a/solution.py
+++ b/solution.py
@@ -94,7 +94,12 @@
     frames = build_frames(slip_rate, onsets)
     rates = jnp.einsum("fnk,k->nf", frames, taps, preferred_element_type=jnp.float32)
     local_rate = moment[:, None, :] * rates[None, :, :]
-    moment_rate = lax.all_gather(local_rate, ("gx", "gy", "gz"), axis=2, tiled=True)
+    moment_rate = jnp.concatenate(
+        lax.all_to_all(
+            jnp.stack([local_rate] * lax.axis_size(("gx", "gy", "gz"))), ("gx", "gy", "gz"), 0, 0
+        ),
+        axis=2,
+    )
     width_x, width_y, width_z = buoyancy.shape
     local_x = cells[0] - lax.axis_index("gx") * width_x
     local_y = cells[1] - lax.axis_index("gy") * width_y

time: 2120 us -> 1420 us (0.67)
  blocking collectives: 681 us -> 0 us
  local copies, waits for them, and re-layouts: 150 us -> 186 us
  starting transfers between devices: 483 us -> 447 us
    all_gather x1 -> x0, blocking collectives: 681 us -> none  [on_device(): lax.all_gather(local_rate, ('gx', 'gy', 'gz'), axis=2, tiled=True)]
    ppermute x96, starting transfers between devices: 233 us -> 189 us  [with_halo(): lax.ppermute(lax.slice_in_dim(block, 0, width, axis=dim), axis, backward)]
    ppermute x96, waiting for transfers between devices: 441 us -> 401 us  [with_halo(): lax.ppermute(lax.slice_in_dim(block, block.shape[dim] - width, None, axis...]
  transfers between devices with their start and end apart: 192 -> 193, of which waited for: 144 -> 145; matrix products, arithmetic and copies ran while one was open for 0% -> 0% of each run, Pallas kernels for 0% -> 0%
where the time goes in v1:
time: 1420 us; the launch traced here: 1410 us
  waiting for transfers between devices  492 us (35%)
  starting transfers between devices  447 us (31%)
  other arithmetic  282 us (20%)
  local copies, waits for them, and re-layouts  186 us (13%)
    ppermute x96, waiting for transfers between devices, with_halo(): lax.ppermute(lax.slice_in_dim(block, block.shape[dim] - width, None, axis...  401 us
    while x144, other arithmetic  252 us
    ppermute x96, starting transfers between devices, with_halo(): lax.ppermute(lax.slice_in_dim(block, block.shape[dim] - width, None, axis...  243 us
    ppermute x96, starting transfers between devices, with_halo(): lax.ppermute(lax.slice_in_dim(block, 0, width, axis=dim), axis, backward)  189 us
    ppermute x96, waiting for transfers between devices, with_halo(): lax.ppermute(lax.slice_in_dim(block, 0, width, axis=dim), axis, backward)  69.7 us
    another operation x16, local copies, waits for them, and re-layouts  46.3 us
    another operation x16, local copies, waits for them, and re-layouts, stress_update(): jnp.stack([normal_x, normal_y, normal_z, shear_xy, shear_xz, shear_yz])  44.1 us
  transfers between devices with their start and end apart: 193, of which 145 were waited for; matrix products, arithmetic and copies ran while one was open for 0% of the time, Pallas kernels for 0%

profile of v1, /device:TPU:30, one launch (start us, length us, event | category | flops | bytes accessed | tf_op | source)
XLA Modules:
  0.0 1412.2 jit_solution(12417311000694409237)
XLA Ops:
  1.3 23.4 %while.17 = (s32[]{:T(128)}, bf16[8,4096]{1,0:T(8,128)(2,1)}, s32[8,2]{0,1:T(2,128)S(1)}, bf16[8,1472]{1,0:T(8,128)(2,1)S(1)}, s32[]{:T(128)}, /*index=5*/s32[]{:T(128)}) while((s32[]{:T(128)}, bf16[8,4096]{1,0:T(8,128)(2,1)}, s32[8,2]{0,1:T(2,128)S(1)}, bf16[8,1472]{1,0:T(8,128)(2,1)S(1)}, s32[]{:T(128)}, /*index=5*/s32[]{:T(128)}) %tuple.93), condition=%wide.while_cond, body=%wide.while_body.sunk | while | flops 2 | bytes 11889 | solution.py:86
  25.8 24.0 %gather_fusion = bf16[8192,8]{1,0:T(8,128)(2,1)S(1)} fusion(bf16[8,1472]{0,1:T(8,128)(2,1)S(1)} %copy.63, s32[8192]{0:T(1024)S(1)} %broadcast_clamp_fusion), kind=kCustom, calls=%fused_computation | custom fusion | bytes 294912 | tf_op jit(solution)/shard_map/vmap()/gather | solution.py:86
  53.4 5.5 reshape.160
  59.0 14.4 %all-to-all-start = ((f32[256,1,768]{2,1,0:T(1,128)}), f32[256,1,768]{2,1,0:T(1,128)S(1)}, u32[]{:S(2)}, u32[]{:S(2)}) async-start(f32[256,1,768]{2,1,0:T(1,128)} %reshape.160), calls=%async_computation | async-start | bytes 1572864 | tf_op jit(solution)/shard_map/all_to_all | solution.py:98
  76.2 21.1 %all-to-all-done = f32[256,1,768]{2,1,0:T(1,128)S(1)} async-done(((f32[256,1,768]{2,1,0:T(1,128)}), f32[256,1,768]{2,1,0:T(1,128)S(1)}, u32[]{:S(2)}, u32[]{:S(2)}) %all-to-all-start) | async-done | bytes 786464 | tf_op jit(solution)/shard_map/all_to_all | solution.py:98
  104.1 5.8 copy_bitcast_fusion
  110.0 16.9 %copy.66 = f32[6,16,2048]{0,2,1:T(8,128)} copy(f32[6,16,2048]{1,2,0:T(8,128)} %copy_bitcast_fusion) | data formatting | bytes 1572864 | tf_op jit(solution)/shard_map/while | solution.py:131
  126.9 1281.7 %while.16 = (s32[]{:T(128)}, f32[3,4,8,256]{3,2,1,0:T(8,128)S(1)}, f32[6,4,8,256]{0,3,2,1:T(8,128)}, f32[4,8,256]{2,1,0:T(8,128)S(1)}, f32[4,8,256]{2,1,0:T(8,12...) while((s32[]{:T(128)}, f32[3,4,8,256]{3,2,1,0:T(8,128)S(1)}, ...), condition=%wide.region_2.3_spmd, body=%wide.region_0.2_spmd.sunk | while | flops 2405409 | bytes 10088273 | solution.py:131
  145.2 4.8 collective-permute-done.3
  157.1 4.4 collective-permute-done.5
  187.0 4.4 collective-permute-done.11
  195.3 15.0 %scatter_custom_fusion.5 = f32[6,8192]{0,1:T(8,128)} fusion(f32[6,8192]{0,1:T(8,128)} %bitcast.181, s32[2048]{0:T(1024)S(1)} %broadcast_select_fusion.5, f32[6,16,2048]{0,2,1:T(8,128)} %get-tuple-element.489, s32[]{:T(128)} %constant.82.clone.1..sunk, s32[]{:T(128)S(6)} %copy.91, f32[]{:T(128)} %constant.80.clone.1..sunk), kind=kCustom, calls=%fused_computation.3.clone.1 | custom fusion | flops 24576 | bytes 1246212 | tf_op jit(solution)/shard_map/while
  239.8 4.4 collective-permute-done.5
  268.3 4.4 collective-permute-done.11
  276.5 15.0 %scatter_custom_fusion.5 = f32[6,8192]{0,1:T(8,128)} fusion(f32[6,8192]{0,1:T(8,128)} %bitcast.181, s32[2048]{0:T(1024)S(1)} %broadcast_select_fusion.5, f32[6,16,2048]{0,2,1:T(8,128)} %get-tuple-element.489, s32[]{:T(128)} %constant.82.clone.1..sunk, s32[]{:T(128)S(6)} %copy.91, f32[]{:T(128)} %constant.80.clone.1..sunk), kind=kCustom, calls=%fused_computation.3.clone.1 | custom fusion | flops 24576 | bytes 1246212 | tf_op jit(solution)/shard_map/while
  319.6 4.4 collective-permute-done.5
  348.1 4.4 collective-permute-done.11
  356.3 15.0 %scatter_custom_fusion.5 = f32[6,8192]{0,1:T(8,128)} fusion(f32[6,8192]{0,1:T(8,128)} %bitcast.181, s32[2048]{0:T(1024)S(1)} %broadcast_select_fusion.5, f32[6,16,2048]{0,2,1:T(8,128)} %get-tuple-element.489, s32[]{:T(128)} %constant.82.clone.1..sunk, s32[]{:T(128)S(6)} %copy.91, f32[]{:T(128)} %constant.80.clone.1..sunk), kind=kCustom, calls=%fused_computation.3.clone.1 | custom fusion | flops 24576 | bytes 1246212 | tf_op jit(solution)/shard_map/while
  399.4 4.4 collective-permute-done.5
  427.9 4.4 collective-permute-done.11
  436.1 15.0 %scatter_custom_fusion.5 = f32[6,8192]{0,1:T(8,128)} fusion(f32[6,8192]{0,1:T(8,128)} %bitcast.181, s32[2048]{0:T(1024)S(1)} %broadcast_select_fusion.5, f32[6,16,2048]{0,2,1:T(8,128)} %get-tuple-element.489, s32[]{:T(128)} %constant.82.clone.1..sunk, s32[]{:T(128)S(6)} %copy.91, f32[]{:T(128)} %constant.80.clone.1..sunk), kind=kCustom, calls=%fused_computation.3.clone.1 | custom fusion | flops 24576 | bytes 1246212 | tf_op jit(solution)/shard_map/while
  479.2 4.4 collective-permute-done.5
  507.6 4.4 collective-permute-done.11
  515.9 15.0 %scatter_custom_fusion.5 = f32[6,8192]{0,1:T(8,128)} fusion(f32[6,8192]{0,1:T(8,128)} %bitcast.181, s32[2048]{0:T(1024)S(1)} %broadcast_select_fusion.5, f32[6,16,2048]{0,2,1:T(8,128)} %get-tuple-element.489, s32[]{:T(128)} %constant.82.clone.1..sunk, s32[]{:T(128)S(6)} %copy.91, f32[]{:T(128)} %constant.80.clone.1..sunk), kind=kCustom, calls=%fused_computation.3.clone.1 | custom fusion | flops 24576 | bytes 1246212 | tf_op jit(solution)/shard_map/while
  559.0 4.4 collective-permute-done.5
  587.4 4.4 collective-permute-done.11
  595.7 15.0 %scatter_custom_fusion.5 = f32[6,8192]{0,1:T(8,128)} fusion(f32[6,8192]{0,1:T(8,128)} %bitcast.181, s32[2048]{0:T(1024)S(1)} %broadcast_select_fusion.5, f32[6,16,2048]{0,2,1:T(8,128)} %get-tuple-element.489, s32[]{:T(128)} %constant.82.clone.1..sunk, s32[]{:T(128)S(6)} %copy.91, f32[]{:T(128)} %constant.80.clone.1..sunk), kind=kCustom, calls=%fused_computation.3.clone.1 | custom fusion | flops 24576 | bytes 1246212 | tf_op jit(solution)/shard_map/while
  638.8 4.4 collective-permute-done.5
  667.2 4.4 collective-permute-done.11
  675.5 15.0 %scatter_custom_fusion.5 = f32[6,8192]{0,1:T(8,128)} fusion(f32[6,8192]{0,1:T(8,128)} %bitcast.181, s32[2048]{0:T(1024)S(1)} %broadcast_select_fusion.5, f32[6,16,2048]{0,2,1:T(8,128)} %get-tuple-element.489, s32[]{:T(128)} %constant.82.clone.1..sunk, s32[]{:T(128)S(6)} %copy.91, f32[]{:T(128)} %constant.80.clone.1..sunk), kind=kCustom, calls=%fused_computation.3.clone.1 | custom fusion | flops 24576 | bytes 1246212 | tf_op jit(solution)/shard_map/while
  718.6 4.4 collective-permute-done.5
  755.3 15.0 %scatter_custom_fusion.5 = f32[6,8192]{0,1:T(8,128)} fusion(f32[6,8192]{0,1:T(8,128)} %bitcast.181, s32[2048]{0:T(1024)S(1)} %broadcast_select_fusion.5, f32[6,16,2048]{0,2,1:T(8,128)} %get-tuple-element.489, s32[]{:T(128)} %constant.82.clone.1..sunk, s32[]{:T(128)S(6)} %copy.91, f32[]{:T(128)} %constant.80.clone.1..sunk), kind=kCustom, calls=%fused_computation.3.clone.1 | custom fusion | flops 24576 | bytes 1246212 | tf_op jit(solution)/shard_map/while
  798.4 4.4 collective-permute-done.5
  835.1 15.0 %scatter_custom_fusion.5 = f32[6,8192]{0,1:T(8,128)} fusion(f32[6,8192]{0,1:T(8,128)} %bitcast.181, s32[2048]{0:T(1024)S(1)} %broadcast_select_fusion.5, f32[6,16,2048]{0,2,1:T(8,128)} %get-tuple-element.489, s32[]{:T(128)} %constant.82.clone.1..sunk, s32[]{:T(128)S(6)} %copy.91, f32[]{:T(128)} %constant.80.clone.1..sunk), kind=kCustom, calls=%fused_computation.3.clone.1 | custom fusion | flops 24576 | bytes 1246212 | tf_op jit(solution)/shard_map/while
  878.2 4.4 collective-permute-done.5
  914.9 15.0 %scatter_custom_fusion.5 = f32[6,8192]{0,1:T(8,128)} fusion(f32[6,8192]{0,1:T(8,128)} %bitcast.181, s32[2048]{0:T(1024)S(1)} %broadcast_select_fusion.5, f32[6,16,2048]{0,2,1:T(8,128)} %get-tuple-element.489, s32[]{:T(128)} %constant.82.clone.1..sunk, s32[]{:T(128)S(6)} %copy.91, f32[]{:T(128)} %constant.80.clone.1..sunk), kind=kCustom, calls=%fused_computation.3.clone.1 | custom fusion | flops 24576 | bytes 1246212 | tf_op jit(solution)/shard_map/while
  958.0 4.4 collective-permute-done.5
  994.7 15.0 %scatter_custom_fusion.5 = f32[6,8192]{0,1:T(8,128)} fusion(f32[6,8192]{0,1:T(8,128)} %bitcast.181, s32[2048]{0:T(1024)S(1)} %broadcast_select_fusion.5, f32[6,16,2048]{0,2,1:T(8,128)} %get-tuple-element.489, s32[]{:T(128)} %constant.82.clone.1..sunk, s32[]{:T(128)S(6)} %copy.91, f32[]{:T(128)} %constant.80.clone.1..sunk), kind=kCustom, calls=%fused_computation.3.clone.1 | custom fusion | flops 24576 | bytes 1246212 | tf_op jit(solution)/shard_map/while
  1037.8 4.4 collective-permute-done.5
  1074.5 15.0 %scatter_custom_fusion.5 = f32[6,8192]{0,1:T(8,128)} fusion(f32[6,8192]{0,1:T(8,128)} %bitcast.181, s32[2048]{0:T(1024)S(1)} %broadcast_select_fusion.5, f32[6,16,2048]{0,2,1:T(8,128)} %get-tuple-element.489, s32[]{:T(128)} %constant.82.clone.1..sunk, s32[]{:T(128)S(6)} %copy.91, f32[]{:T(128)} %constant.80.clone.1..sunk), kind=kCustom, calls=%fused_computation.3.clone.1 | custom fusion | flops 24576 | bytes 1246212 | tf_op jit(solution)/shard_map/while
  1117.6 4.4 collective-permute-done.5
  1154.3 15.0 %scatter_custom_fusion.5 = f32[6,8192]{0,1:T(8,128)} fusion(f32[6,8192]{0,1:T(8,128)} %bitcast.181, s32[2048]{0:T(1024)S(1)} %broadcast_select_fusion.5, f32[6,16,2048]{0,2,1:T(8,128)} %get-tuple-element.489, s32[]{:T(128)} %constant.82.clone.1..sunk, s32[]{:T(128)S(6)} %copy.91, f32[]{:T(128)} %constant.80.clone.1..sunk), kind=kCustom, calls=%fused_computation.3.clone.1 | custom fusion | flops 24576 | bytes 1246212 | tf_op jit(solution)/shard_map/while
  1197.4 4.4 collective-permute-done.5
  1234.1 15.0 %scatter_custom_fusion.5 = f32[6,8192]{0,1:T(8,128)} fusion(f32[6,8192]{0,1:T(8,128)} %bitcast.181, s32[2048]{0:T(1024)S(1)} %broadcast_select_fusion.5, f32[6,16,2048]{0,2,1:T(8,128)} %get-tuple-element.489, s32[]{:T(128)} %constant.82.clone.1..sunk, s32[]{:T(128)S(6)} %copy.91, f32[]{:T(128)} %constant.80.clone.1..sunk), kind=kCustom, calls=%fused_computation.3.clone.1 | custom fusion | flops 24576 | bytes 1246212 | tf_op jit(solution)/shard_map/while
  1277.2 4.4 collective-permute-done.5
  1313.9 15.0 %scatter_custom_fusion.5 = f32[6,8192]{0,1:T(8,128)} fusion(f32[6,8192]{0,1:T(8,128)} %bitcast.181, s32[2048]{0:T(1024)S(1)} %broadcast_select_fusion.5, f32[6,16,2048]{0,2,1:T(8,128)} %get-tuple-element.489, s32[]{:T(128)} %constant.82.clone.1..sunk, s32[]{:T(128)S(6)} %copy.91, f32[]{:T(128)} %constant.80.clone.1..sunk), kind=kCustom, calls=%fused_computation.3.clone.1 | custom fusion | flops 24576 | bytes 1246212 | tf_op jit(solution)/shard_map/while
  1357.0 4.4 collective-permute-done.5
  1393.7 15.0 %scatter_custom_fusion.5 = f32[6,8192]{0,1:T(8,128)} fusion(f32[6,8192]{0,1:T(8,128)} %bitcast.181, s32[2048]{0:T(1024)S(1)} %broadcast_select_fusion.5, f32[6,16,2048]{0,2,1:T(8,128)} %get-tuple-element.489, s32[]{:T(128)} %constant.82.clone.1..sunk, s32[]{:T(128)S(6)} %copy.91, f32[]{:T(128)} %constant.80.clone.1..sunk), kind=kCustom, calls=%fused_computation.3.clone.1 | custom fusion | flops 24576 | bytes 1246212 | tf_op jit(solution)/shard_map/while
  (882 shorter events, 973.1 us)
Async XLA Ops:
  59.0 38.3 %all-to-all-start = ((f32[256,1,768]{2,1,0:T(1,128)}), f32[256,1,768]{2,1,0:T(1,128)S(1)}, u32[]{:S(2)}, u32[]{:S(2)}) async-start(f32[256,1,768]{2,1,0:T(1,128)} %reshape.160), calls=%async_computation | async-start | bytes 1572864 | tf_op jit(solution)/shard_map/all_to_all | solution.py:98
  131.8 8.1 collective-permute-start.1
  152.9 8.6 collective-permute-start.5
  164.5 7.8 collective-permute-start.7
  215.1 8.1 collective-permute-start.1
  235.6 8.6 collective-permute-start.5
  247.1 7.8 collective-permute-start.7
  296.3 8.1 collective-permute-start.1
  315.4 8.6 collective-permute-start.5
  326.9 7.8 collective-permute-start.7
  376.1 8.1 collective-permute-start.1
  395.2 8.6 collective-permute-start.5
  406.7 7.8 collective-permute-start.7
  455.9 8.1 collective-permute-start.1
  475.0 8.6 collective-permute-start.5
  486.5 7.8 collective-permute-start.7
  535.7 8.1 collective-permute-start.1
  554.8 8.6 collective-permute-start.5
  566.3 7.8 collective-permute-start.7
  615.5 8.1 collective-permute-start.1
  634.6 8.6 collective-permute-start.5
  646.1 7.8 collective-permute-start.7
  695.3 8.1 collective-permute-start.1
  714.4 8.6 collective-permute-start.5
  725.9 7.8 collective-permute-start.7
  775.1 8.1 collective-permute-start.1
  794.2 8.6 collective-permute-start.5
  805.7 7.8 collective-permute-start.7
  854.9 8.1 collective-permute-start.1
  874.0 8.6 collective-permute-start.5
  885.5 7.8 collective-permute-start.7
  934.7 8.1 collective-permute-start.1
  953.8 8.6 collective-permute-start.5
  965.3 7.8 collective-permute-start.7
  1014.5 8.1 collective-permute-start.1
  1033.6 8.6 collective-permute-start.5
  1045.1 7.8 collective-permute-start.7
  1094.3 8.1 collective-permute-start.1
  1113.4 8.6 collective-permute-start.5
  1124.9 7.8 collective-permute-start.7
  1174.1 8.1 collective-permute-start.1
  1193.2 8.6 collective-permute-start.5
  1204.7 7.8 collective-permute-start.7
  1253.9 8.1 collective-permute-start.1
  1273.0 8.6 collective-permute-start.5
  1284.5 7.8 collective-permute-start.7
  1333.7 8.1 collective-permute-start.1
  1352.8 8.6 collective-permute-start.5
  (155 other events, 1033.8 us)
